TPU v7x, 256 devices: a whole 4x4x8 slice. The times are simulated.
256 devices in a mesh: dp: 32 (over y, z), expert: 8 (over x, core).
Axes of the slice: x: 4, y: 4, z: 8, core: 2. Of those that a mesh axis runs over, the one named last changes fastest.
Arguments:
- master: float32 [8, 4096, 1536], P('expert', 'dp'), may hold values from -0.109375 to 0.109375
- moment_one: float32 [8, 4096, 1536], P('expert', 'dp'), may hold values from -1.5 to 1.5
- moment_two: float32 [8, 4096, 1536], P('expert', 'dp'), may hold values from 0.0001 to 0.003
- saved_rows: bfloat16 [8, 12288, 1536], P('expert', 'dp'), may hold values from -6 to 6
- saved_grads: bfloat16 [8, 12288, 4096], P('expert', 'dp'), may hold values from -0.109375 to 0.109375
- slot_rows: bfloat16 [32768, 2, 1536], P(('dp', 'expert')), may hold values from -6 to 6
- routes: int32 [32768, 2], P(('dp', 'expert')), may hold values from 0 to 7, all different within a row; in each aligned block of 128 rows (0 to 127, 128 to 255, ...) at most 40 rows name the same one
- gates: float32 [32768, 2], P(('dp', 'expert')), may hold values from 0.1 to 1
Outputs:
- master_new: float32 [8, 4096, 1536], P('expert', 'dp')
- moment_one_new: float32 [8, 4096, 1536], P('expert', 'dp')
- moment_two_new: float32 [8, 4096, 1536], P('expert', 'dp')
- mixed: bfloat16 [32768, 4096], P(('dp', 'expert'))
Inputs may be any that keep to these rules, and one draw needn't show every extreme that they name: `routes`: each token names 2 different experts. Among the 128 tokens of one device (aligned blocks of rows in device order, dp slowest) at most 40 name the same expert, and in some device's block exactly 40 do.
All inputs are finite; a program needn't handle non-finite values.
Results may differ from a plain program's by a relative error of at most 0.034.
Values may be sent and summed in bfloat16 or wider, within the bound.
No kernel may reach another device: no remote copies, remote signals or barrier semaphores. Data moves between devices by JAX's collectives and lax.ppermute only.
A program may use at most 128 MiB of HBM per device.

v0:
```python
import jax
import jax.numpy as jnp
from jax import lax
from jax.sharding import PartitionSpec as P

beta_one = 0.9
beta_two = 0.999
learn_rate = 0.002
tiny_eps = 1e-08
steps_done = 100.0


def adam_update(master, moment_one, moment_two, grad):
    m_new = beta_one * moment_one + (1.0 - beta_one) * grad
    v_new = beta_two * moment_two + (1.0 - beta_two) * grad * grad
    fix_one = 1.0 - beta_one**steps_done
    fix_two = 1.0 - beta_two**steps_done
    step_size = m_new / fix_one / (jnp.sqrt(v_new / fix_two) + tiny_eps)
    return (master - learn_rate * step_size, m_new, v_new)


def slot_places(routes, experts):
    flat = routes.reshape(-1)
    onehot = (flat[:, None] == jnp.arange(experts, dtype=jnp.int32)[None, :]).astype(jnp.int32)
    place = jnp.sum((jnp.cumsum(onehot, axis=0) - onehot) * onehot, axis=1)
    return (flat, place)


def send_back(results):
    return lax.all_to_all(results, "expert", split_axis=0, concat_axis=0, tiled=True)


def body(master, moment_one, moment_two, saved_rows, saved_grads, slot_rows, routes, gates):
    rows_here = saved_rows[0]
    grads_here = saved_grads[0]
    grad = lax.psum_scatter(
        lax.dot_general(
            grads_here, rows_here, (((0,), (0,)), ((), ())), preferred_element_type=jnp.float32
        ).astype(jnp.bfloat16),
        "dp",
        scatter_dimension=0,
        tiled=True,
    ).astype(jnp.float32)
    master_new, m_new, v_new = adam_update(master[0], moment_one[0], moment_two[0], grad)
    weights_shard = master_new.astype(jnp.bfloat16)
    experts = lax.axis_size("expert")
    tok_count, top_count, width = slot_rows.shape
    capacity = tok_count * top_count * 5 // (4 * experts)
    flat, place = slot_places(routes, experts)
    outgoing = (
        jnp.zeros((experts, capacity, width), jnp.bfloat16)
        .at[flat, place]
        .set(slot_rows.reshape(-1, width))
    )
    weights = lax.all_gather(weights_shard, "dp", axis=0, tiled=True)
    out_width = weights.shape[0]
    received = lax.all_to_all(outgoing, "expert", split_axis=0, concat_axis=0, tiled=True)
    sources, count, _ = received.shape
    product = lax.dot_general(
        received.reshape(-1, width),
        weights,
        (((1,), (1,)), ((), ())),
        preferred_element_type=jnp.float32,
    )
    returned = send_back(product.astype(jnp.bfloat16).reshape(sources, count, out_width))
    out_width = returned.shape[2]
    picked = returned[flat, place].astype(jnp.float32).reshape(tok_count, top_count, out_width)
    mixed = jnp.sum(picked * gates[:, :, None], axis=1).astype(jnp.bfloat16)
    return (master_new[None], m_new[None], v_new[None], mixed)


def solution(mesh):
    placed = (
        P("expert", "dp", None),
        P("expert", "dp", None),
        P("expert", "dp", None),
        P("expert", "dp", None),
        P("expert", "dp", None),
        P(("dp", "expert"), None, None),
        P(("dp", "expert"), None),
        P(("dp", "expert"), None),
    )
    return jax.shard_map(
        body,
        mesh=mesh,
        in_specs=placed,
        out_specs=(
            P("expert", "dp", None),
            P("expert", "dp", None),
            P("expert", "dp", None),
            P(("dp", "expert"), None),
        ),
        check_vma=False,
    )
```

profile of v0, /device:TPU:1, one launch (start us, length us, event | category | flops | bytes accessed | tf_op | source)
XLA Modules:
  0.0 461.5 jit_solution(4875685492731966594)
XLA Ops:
  7.2 0.0 copy-start
  7.2 0.0 reduce-scatter.2.cloned.1.call-start
  7.2 1.8 copy-done
  9.1 10.9 %convolution_convert_fusion = bf16[4096,1536]{1,0:T(8,128)(2,1)} fusion(bf16[1,384,4096]{2,1,0:T(8,128)(2,1)S(1)} %copy-done, bf16[1,384,1536]{2,1,0:T(8,128)(2,1)} %param.11), kind=kOutput, calls=%fused_computation.2 | convolution fusion | flops 4838129664 | bytes 16908288 | tf_op jit(solution)/shard_map/dot_general | solution.py:37
  19.9 0.0 reduce-scatter.2.cloned.1.call-update
  20.0 0.0 copy-start.1
  20.0 0.0 all-gather.2.cloned.1.call-start
  20.0 238.8 %reduce-scatter.2.cloned.1.call-done = bf16[128,1536]{1,0:T(8,128)(2,1)} async-done(((bf16[4096,1536]{1,0:T(8,128)(2,1)}), bf16[128,1536]{1,0:T(8,128)(2,1)}) %reduce-scatter.2.cloned.1.call-update) | async-done | bytes 393232 | tf_op jit(solution)/shard_map/reduce_scatter | solution.py:36
  258.8 3.8 fusion.10
  262.6 0.0 all-gather.2.cloned.1.call-update
  262.6 0.0 copy-done.1
  262.6 0.1 copy.13
  262.8 0.1 reshape.87
  262.9 0.1 eq.29
  263.0 0.1 eq.25
  263.2 0.6 reduce-window.6
  263.8 0.2 slice_reduce_fusion
  264.0 3.0 reshape.101
  267.0 0.1 fusion.7
  267.1 1.0 broadcast_in_dim.21
  268.1 42.2 %scatter_fusion = bf16[8,40,1536]{2,1,0:T(8,128)(2,1)} fusion(bf16[8,40,1536]{2,1,0:T(8,128)(2,1)} %broadcast_in_dim.21, s32[256]{0:T(256)S(1)} %bitcast.44, bf16[256,1536]{1,0:T(8,128)(2,1)} %reshape.101), kind=kCustom, calls=%fused_computation.1 | custom fusion | bytes 2361344 | tf_op jit(solution)/shard_map/scatter | solution.py:53
  310.3 23.0 %all_to_all.10 = bf16[8,40,1536]{2,1,0:T(8,128)(2,1)} all-to-all(bf16[8,40,1536]{2,1,0:T(8,128)(2,1)} %scatter_fusion), channel_id=1, replica_groups=mesh['dp'=32,'expert'=8] {'expert'}, dimensions={0} | all-to-all | bytes 1966080 | tf_op jit(solution)/shard_map/all_to_all | solution.py:57
  333.3 50.5 %all-gather.2.cloned.1.call-done = bf16[4096,1536]{1,0:T(8,128)(2,1)} async-done(((bf16[128,1536]{1,0:T(8,128)(2,1)}), bf16[4096,1536]{1,0:T(8,128)(2,1)}) %all-gather.2.cloned.1.call-update) | async-done | bytes 12582928 | tf_op jit(solution)/shard_map/all_gather | solution.py:55
  383.9 10.6 %convolution_convert_fusion.1 = bf16[320,4096]{1,0:T(8,128)(2,1)} fusion(bf16[320,1536]{1,0:T(8,128)(2,1)} %bitcast.46, bf16[4096,1536]{1,0:T(8,128)(2,1)} %all-gather.2.cloned.1.call-done), kind=kOutput, calls=%fused_computation.3 | convolution fusion | flops 4027842560 | bytes 16187392 | tf_op jit(solution)/shard_map/dot_general | solution.py:59
  394.5 0.0 copy-start.2
  394.5 5.8 %all-to-all-start.1 = ((bf16[8,40,4096]{2,1,0:T(8,128)(2,1)}), bf16[8,40,4096]{2,1,0:T(8,128)(2,1)}, u32[]{:S(2)}, u32[]{:S(2)}) async-start(bf16[8,40,4096]{2,1,0:T(8,128)(2,1)} %bitcast.45), calls=%async_computation.2 | async-start | bytes 5242880 | tf_op jit(solution)/shard_map/all_to_all | solution.py:30
  400.3 0.0 copy-done.2
  400.3 0.1 copy.16
  400.4 31.8 %all-to-all-done.1 = bf16[8,40,4096]{2,1,0:T(8,128)(2,1)} async-done(((bf16[8,40,4096]{2,1,0:T(8,128)(2,1)}), bf16[8,40,4096]{2,1,0:T(8,128)(2,1)}, u32[]{:S(2)}, u32[]{:S(2)}) %all-to-all-start.1) | async-done | bytes 2621472 | tf_op jit(solution)/shard_map/all_to_all | solution.py:30
  432.2 7.3 %gather_fusion = bf16[256,4096]{1,0:T(8,128)(2,1)} fusion(bf16[8,40,4096]{2,1,0:T(8,128)(2,1)} %all-to-all-done.1, s32[256]{0:T(256)S(1)} %bitcast.43), kind=kCustom, calls=%fused_computation | custom fusion | bytes 4196352 | tf_op jit(solution)/shard_map/gather | solution.py:67
  439.6 5.4 %reshape.92 = f32[128,2,4096]{2,1,0:T(2,128)} reshape(bf16[256,4096]{1,0:T(8,128)(2,1)} %gather_fusion) | data formatting | bytes 6291456 | tf_op jit(solution)/shard_map/convert_element_type | solution.py:67
  445.0 9.6 %multiply_reduce_fusion = bf16[128,4096]{1,0:T(8,128)(2,1)} fusion(f32[128,2,4096]{2,1,0:T(2,128)} %reshape.92, f32[128,2]{1,0:T(8,128)S(1)} %copy.16), kind=kLoop, calls=%fused_computation.4 | loop fusion | flops 1572864 | bytes 5243904 | tf_op jit(solution)/shard_map/reduce_sum | solution.py:68
  (4 shorter events, 0.1 us)
Async XLA Ops:
  7.2 1.9 copy-start
  7.2 251.6 %reduce-scatter.2.cloned.1.call-start = ((), (), s32[]{:S(2)}) async-start(), calls=%async_computation.3 | async-start | bytes 12976128 | tf_op jit(solution)/shard_map/reduce_scatter | solution.py:36
  20.0 242.7 %copy-start.1 = (s32[128,2]{0,1:T(2,128)S(1)}, s32[128,2]{0,1:T(2,128)}, u32[]{:S(2)}) copy-start(s32[128,2]{0,1:T(2,128)} %param.14) | copy-start | bytes 3076
  20.0 363.9 %all-gather.2.cloned.1.call-start = ((), (), s32[]{:S(2)}) async-start(), calls=%async_computation.4 | async-start | bytes 12976128 | tf_op jit(solution)/shard_map/all_gather | solution.py:55
  394.5 5.8 %copy-start.2 = (f32[128,2]{0,1:T(2,128)S(1)}, f32[128,2]{0,1:T(2,128)}, u32[]{:S(2)}) copy-start(f32[128,2]{0,1:T(2,128)} %param.15) | copy-start | bytes 3076
  394.5 37.7 %all-to-all-start.1 = ((bf16[8,40,4096]{2,1,0:T(8,128)(2,1)}), bf16[8,40,4096]{2,1,0:T(8,128)(2,1)}, u32[]{:S(2)}, u32[]{:S(2)}) async-start(bf16[8,40,4096]{2,1,0:T(8,128)(2,1)} %bitcast.45), calls=%async_computation.2 | async-start | bytes 5242880 | tf_op jit(solution)/shard_map/all_to_all | solution.py:30
Sparse Core Ops, SparseCore 0:
  20.1 238.6 reduce-scatter.1
  262.7 121.0 all-gather.1
where the time goes:
time: 463 us; the launch traced here: 461 us
  waiting for transfers between devices  321 us (69%)
  local copies, waits for them, and re-layouts  61.6 us (13%)
  blocking collectives  23 us (5%)
  matrix products  21.5 us (5%)
  other arithmetic  14.2 us (3%)
  between operations  14.1 us (3%)
  starting transfers between devices  5.87 us (1%)
    reduce_scatter x1, waiting for transfers between devices, body(): lax.psum_scatter(lax.dot_general(grads_here, rows_here, (((0,), (0,)), ((...  239 us
    all_gather x1, waiting for transfers between devices, body(): weights = lax.all_gather(weights_shard, 'dp', axis=0, tiled=True)  50.5 us
    scatter x1, local copies, waits for them, and re-layouts, body(): outgoing = jnp.zeros((experts, capacity, width), jnp.bfloat16).at[flat, p...  42.2 us
    all_to_all x1, waiting for transfers between devices, send_back(): lax.all_to_all(results, 'expert', split_axis=0, concat_axis=0, tiled=True)  31.8 us
    all_to_all x1, blocking collectives, body(): lax.all_to_all(outgoing, 'expert', split_axis=0, concat_axis=0, tiled=True)  23 us
    dot_general x1, matrix products, body(): lax.dot_general(grads_here, rows_here, (((0,), (0,)), ((), ())), preferre...  10.9 us
    dot_general x1, matrix products, body(): lax.dot_general(received.reshape(-1, width), weights, (((1,), (1,)), ((),...  10.6 us
    reduce_sum x1, other arithmetic, body(): mixed = jnp.sum(picked * gates[:, :, None], axis=1).astype(jnp.bfloat16)  9.64 us
  transfers between devices with their start and end apart: 3, of which 3 were waited for; matrix products, arithmetic and copies ran while one was open for 10% of the time, Pallas kernels for 0%

commit v1 on v0

--- a/solution.py
+++ b/solution.py
@@ -52,7 +52,9 @@
         .at[flat, place]
         .set(slot_rows.reshape(-1, width))
     )
-    weights = lax.all_gather(weights_shard, "dp", axis=0, tiled=True)
+    weights = jnp.concatenate(
+        lax.all_to_all(jnp.stack([weights_shard] * lax.axis_size("dp")), "dp", 0, 0), axis=0
+    )
     out_width = weights.shape[0]
     received = lax.all_to_all(outgoing, "expert", split_axis=0, concat_axis=0, tiled=True)
     sources, count, _ = received.shape

time: 463 us -> 630 us (1.36)
  blocking collectives: 23 us -> 273 us
  waiting for transfers between devices: 321 us -> 216 us
  starting transfers between devices: 5.87 us -> 21 us
  local copies, waits for them, and re-layouts: 61.6 us -> 68 us
    all_to_all x1, blocking collectives: 23 us -> 273 us  [body(): lax.all_to_all(jnp.stack([weights_shard] * lax.axis_size('dp')), 'dp', 0, 0)]
    reduce_scatter x1, waiting for transfers between devices: 239 us -> 184 us  [body(): lax.psum_scatter(lax.dot_general(grads_here, rows_here, (((0,), (0,)), ((...]
    all_gather x1 -> x0, waiting for transfers between devices: 50.5 us -> none  [body(): weights = lax.all_gather(weights_shard, 'dp', axis=0, tiled=True)]
    all_to_all x1, starting transfers between devices: 5.79 us -> 14.2 us  [send_back(): lax.all_to_all(results, 'expert', split_axis=0, concat_axis=0, tiled=True)]
    all_to_all x0 -> x1, starting transfers between devices: none -> 6.82 us  [body(): lax.all_to_all(outgoing, 'expert', split_axis=0, concat_axis=0, tiled=True)]
  transfers between devices with their start and end apart: 3 -> 3, of which waited for: 3 -> 2; matrix products, arithmetic and copies ran while one was open for 10% -> 8% of each run, Pallas kernels for 0% -> 0%
where the time goes in v1:
time: 630 us; the launch traced here: 628 us
  blocking collectives  273 us (43%)
  waiting for transfers between devices  216 us (34%)
  local copies, waits for them, and re-layouts  68 us (11%)
  matrix products  21.5 us (3%)
  starting transfers between devices  21 us (3%)
  between operations  14.1 us (2%)
  other arithmetic  13.8 us (2%)
    all_to_all x1, blocking collectives, body(): lax.all_to_all(jnp.stack([weights_shard] * lax.axis_size('dp')), 'dp', 0, 0)  273 us
    reduce_scatter x1, waiting for transfers between devices, body(): lax.psum_scatter(lax.dot_general(grads_here, rows_here, (((0,), (0,)), ((...  184 us
    scatter x1, local copies, waits for them, and re-layouts, body(): outgoing = jnp.zeros((experts, capacity, width), jnp.bfloat16).at[flat, p...  42 us
    all_to_all x1, waiting for transfers between devices, send_back(): lax.all_to_all(results, 'expert', split_axis=0, concat_axis=0, tiled=True)  31.8 us
    all_to_all x1, starting transfers between devices, send_back(): lax.all_to_all(results, 'expert', split_axis=0, concat_axis=0, tiled=True)  14.2 us
  transfers between devices with their start and end apart: 3, of which 2 were waited for; matrix products, arithmetic and copies ran while one was open for 8% of the time, Pallas kernels for 0%

profile of v1, /device:TPU:1, one launch (start us, length us, event | category | flops | bytes accessed | tf_op | source)
XLA Modules:
  0.0 627.7 jit_solution(2390573944371875730)
XLA Ops:
  7.2 0.0 copy-start
  7.2 0.0 reduce-scatter.2.cloned.1.call-start
  7.2 1.8 copy-done
  9.1 10.9 %convolution_convert_fusion = bf16[4096,1536]{1,0:T(8,128)(2,1)} fusion(bf16[1,384,4096]{2,1,0:T(8,128)(2,1)S(1)} %copy-done, bf16[1,384,1536]{2,1,0:T(8,128)(2,1)} %param.11), kind=kOutput, calls=%fused_computation.2 | convolution fusion | flops 4838129664 | bytes 16908288 | tf_op jit(solution)/shard_map/dot_general | solution.py:37
  19.9 0.0 copy-start.1
  19.9 0.0 reduce-scatter.2.cloned.1.call-update
  20.0 0.7 copy-done.1
  20.6 0.1 copy.13
  20.7 0.1 reshape.92
  20.9 0.1 eq.29
  21.0 0.1 eq.25
  21.2 0.6 reduce-window.6
  21.8 0.2 slice_reduce_fusion
  22.0 3.0 reshape.107
  25.0 0.1 fusion.7
  25.1 1.0 broadcast_in_dim.21
  26.1 42.0 %scatter_fusion = bf16[8,40,1536]{2,1,0:T(8,128)(2,1)} fusion(bf16[8,40,1536]{2,1,0:T(8,128)(2,1)} %broadcast_in_dim.21, s32[256]{0:T(256)S(1)} %bitcast.45, bf16[256,1536]{1,0:T(8,128)(2,1)} %reshape.107), kind=kCustom, calls=%fused_computation.1 | custom fusion | bytes 2361344 | tf_op jit(solution)/shard_map/scatter | solution.py:53
  68.1 6.8 %all-to-all-start = ((bf16[8,40,1536]{2,1,0:T(8,128)(2,1)}), bf16[8,40,1536]{2,1,0:T(8,128)(2,1)}, u32[]{:S(2)}, u32[]{:S(2)}) async-start(bf16[8,40,1536]{2,1,0:T(8,128)(2,1)} %scatter_fusion), calls=%async_computation.1 | async-start | bytes 1966080 | tf_op jit(solution)/shard_map/all_to_all | solution.py:59
  74.9 184.2 %reduce-scatter.2.cloned.1.call-done = bf16[128,1536]{1,0:T(8,128)(2,1)} async-done(((bf16[4096,1536]{1,0:T(8,128)(2,1)}), bf16[128,1536]{1,0:T(8,128)(2,1)}) %reduce-scatter.2.cloned.1.call-update) | async-done | bytes 393232 | tf_op jit(solution)/shard_map/reduce_scatter | solution.py:36
  259.1 3.5 fusion.10
  262.6 0.0 all-to-all-done
  262.6 5.9 stack.2
  268.5 273.3 %all_to_all.15 = bf16[32,128,1536]{2,1,0:T(8,128)(2,1)} all-to-all(bf16[32,128,1536]{2,1,0:T(8,128)(2,1)} %stack.2), channel_id=1, replica_groups=mesh['dp'=32,'expert'=8] {'dp'}, dimensions={0} | all-to-all | bytes 25165824 | tf_op jit(solution)/shard_map/all_to_all | solution.py:56
  541.7 10.6 %convolution_convert_fusion.1 = bf16[320,4096]{1,0:T(8,128)(2,1)} fusion(bf16[320,1536]{1,0:T(8,128)(2,1)} %bitcast.12, bf16[4096,1536]{1,0:T(8,128)(2,1)} %bitcast.46), kind=kOutput, calls=%fused_computation.3 | convolution fusion | flops 4027842560 | bytes 16187392 | tf_op jit(solution)/shard_map/dot_general | solution.py:61
  552.4 0.0 copy-start.2
  552.4 14.2 %all-to-all-start.2 = ((bf16[8,40,4096]{2,1,0:T(8,128)(2,1)}), bf16[8,40,4096]{2,1,0:T(8,128)(2,1)}, u32[]{:S(2)}, u32[]{:S(2)}) async-start(bf16[8,40,4096]{2,1,0:T(8,128)(2,1)} %bitcast.47), calls=%async_computation.3 | async-start | bytes 5242880 | tf_op jit(solution)/shard_map/all_to_all | solution.py:30
  566.5 0.0 copy-done.2
  566.5 0.1 copy.16
  566.7 31.8 %all-to-all-done.2 = bf16[8,40,4096]{2,1,0:T(8,128)(2,1)} async-done(((bf16[8,40,4096]{2,1,0:T(8,128)(2,1)}), bf16[8,40,4096]{2,1,0:T(8,128)(2,1)}, u32[]{:S(2)}, u32[]{:S(2)}) %all-to-all-start.2) | async-done | bytes 2621472 | tf_op jit(solution)/shard_map/all_to_all | solution.py:30
  598.5 7.3 %gather_fusion = bf16[256,4096]{1,0:T(8,128)(2,1)} fusion(bf16[8,40,4096]{2,1,0:T(8,128)(2,1)} %all-to-all-done.2, s32[256]{0:T(256)S(1)} %bitcast.44), kind=kCustom, calls=%fused_computation | custom fusion | bytes 4196352 | tf_op jit(solution)/shard_map/gather | solution.py:69
  605.8 5.4 reshape.98
  611.3 9.6 %multiply_reduce_fusion = bf16[128,4096]{1,0:T(8,128)(2,1)} fusion(f32[128,2,4096]{2,1,0:T(2,128)} %reshape.98, f32[128,2]{1,0:T(8,128)S(1)} %copy.16), kind=kLoop, calls=%fused_computation.4 | loop fusion | flops 1572864 | bytes 5243904 | tf_op jit(solution)/shard_map/reduce_sum | solution.py:70
  (4 shorter events, 0.1 us)
Async XLA Ops:
  7.2 1.9 copy-start
  7.2 251.9 %reduce-scatter.2.cloned.1.call-start = ((), (), s32[]{:S(2)}) async-start(), calls=%async_computation.4 | async-start | bytes 12976128 | tf_op jit(solution)/shard_map/reduce_scatter | solution.py:36
  19.9 0.7 copy-start.1
  68.1 194.5 %all-to-all-start = ((bf16[8,40,1536]{2,1,0:T(8,128)(2,1)}), bf16[8,40,1536]{2,1,0:T(8,128)(2,1)}, u32[]{:S(2)}, u32[]{:S(2)}) async-start(bf16[8,40,1536]{2,1,0:T(8,128)(2,1)} %scatter_fusion), calls=%async_computation.1 | async-start | bytes 1966080 | tf_op jit(solution)/shard_map/all_to_all | solution.py:59
  552.4 14.2 %copy-start.2 = (f32[128,2]{0,1:T(2,128)S(1)}, f32[128,2]{0,1:T(2,128)}, u32[]{:S(2)}) copy-start(f32[128,2]{0,1:T(2,128)} %param.15) | copy-start | bytes 3076
  552.4 46.1 %all-to-all-start.2 = ((bf16[8,40,4096]{2,1,0:T(8,128)(2,1)}), bf16[8,40,4096]{2,1,0:T(8,128)(2,1)}, u32[]{:S(2)}, u32[]{:S(2)}) async-start(bf16[8,40,4096]{2,1,0:T(8,128)(2,1)} %bitcast.47), calls=%async_computation.3 | async-start | bytes 5242880 | tf_op jit(solution)/shard_map/all_to_all | solution.py:30
Sparse Core Ops, SparseCore 0:
  20.1 238.9 reduce-scatter.1
